TPU v7x, 32 devices: a whole 2x2x4 slice. The times are simulated.
32 devices in a mesh: dp: 4 (over x, core), seq: 2 (over y), head: 4 (over z).
Axes of the slice: x: 2, y: 2, z: 4, core: 2. Of those that a mesh axis runs over, the one named last changes fastest.
Arguments:
- embed: bfloat16 [4, 1024, 1536], P('dp', 'seq', 'head'), may hold values from -6 to 6
- donor_pos: int32 [4, 256], P('dp', 'seq'), may hold values from -1 to 1023, as said below
- acceptor_pos: int32 [4, 256], P('dp', 'seq'), may hold values from -1 to 1023, as said below
- target: bfloat16 [4, 256, 256], P('dp', 'seq'), may hold values from 0 to 4
- donor_w: bfloat16 [1536, 384], P('head'), may hold values from -0.15625 to 0.15625
- acceptor_w: bfloat16 [1536, 384], P('head'), may hold values from -0.15625 to 0.15625
Outputs:
- grad_embed: bfloat16 [4, 1024, 1536], P('dp', 'seq', 'head')
- grad_donor_w: float32 [1536, 384], P('head', 'seq')
- grad_acceptor_w: float32 [1536, 384], P('head', 'seq')
Inputs may be any that keep to these rules, and one draw needn't show every extreme that they name: `donor_pos`: slots k * 128 to (k + 1) * 128 - 1 belong to slab k: they hold one or more positions of k * 512 to (k + 1) * 512 - 1 first, then -1 in the remaining slots. Positions may repeat. `acceptor_pos`: as for donor_pos, drawn independently.
All inputs are finite; a program needn't handle non-finite values.
Results may differ from a plain program's by a relative error of at most 0.02.
Values may be sent and summed in bfloat16 or wider, within the bound.
No kernel may reach another device: no remote copies, remote signals or barrier semaphores. Data moves between devices by JAX's collectives and lax.ppermute only.
A program may use at most 64 MiB of HBM per device.

v0:
```python
import math
import jax
import jax.numpy as jnp
from jax import lax
from jax.sharding import PartitionSpec as P


def site_match(positions, slab_rows, slab_index):
    local_pos = positions - slab_index * slab_rows
    return local_pos[:, :, None] == jnp.arange(slab_rows, dtype=jnp.int32)[None, None, :]


def pair_slope(scores, target, allowed):
    rate = jax.nn.softplus(scores) + 1.0
    return jnp.where(
        allowed, (1.0 - target.astype(jnp.float32) / rate) * jax.nn.sigmoid(scores), 0.0
    ).astype(jnp.bfloat16)


def place_rows(match_bf, values):
    upper = values.astype(jnp.bfloat16)
    lower = (values - upper.astype(jnp.float32)).astype(jnp.bfloat16)
    placed = jnp.einsum("bnr,bnc->brc", match_bf, upper, preferred_element_type=jnp.float32)
    return placed + jnp.einsum("bnr,bnc->brc", match_bf, lower, preferred_element_type=jnp.float32)


def shards(embed, donor_pos, acceptor_pos, target, donor_w, acceptor_w):
    batch, slab_rows, _ = embed.shape
    slab_sites = donor_pos.shape[1]
    width = donor_w.shape[1]
    scale = 1.0 / math.sqrt(width)
    n_seq = lax.axis_size("seq")
    n_head = lax.axis_size("head")
    slab = lax.axis_index("seq")
    sites = slab_sites * n_seq
    target_all = lax.all_gather(target, "seq", axis=1, tiled=True)
    donor_match = site_match(donor_pos, slab_rows, slab).astype(jnp.bfloat16)
    acceptor_match = site_match(acceptor_pos, slab_rows, slab).astype(jnp.bfloat16)
    donor_rows = jnp.einsum(
        "bnr,brc->bnc", donor_match, embed, preferred_element_type=jnp.float32
    ).astype(jnp.bfloat16)
    acceptor_rows = jnp.einsum(
        "bnr,brc->bnc", acceptor_match, embed, preferred_element_type=jnp.float32
    ).astype(jnp.bfloat16)
    donor_part = jnp.einsum(
        "bnc,cp->bnp", donor_rows, donor_w, preferred_element_type=jnp.float32
    ).astype(jnp.bfloat16)
    acceptor_part = jnp.einsum(
        "bnc,cp->bnp", acceptor_rows, acceptor_w, preferred_element_type=jnp.float32
    ).astype(jnp.bfloat16)
    assert slab_sites <= width
    flags = jnp.zeros((batch, 8, width), jnp.bfloat16)
    flags = flags.at[:, 0, :slab_sites].set((donor_pos >= 0).astype(jnp.bfloat16))
    flags = flags.at[:, 1, :slab_sites].set((acceptor_pos >= 0).astype(jnp.bfloat16))
    packed = jnp.concatenate([donor_part, acceptor_part, flags], axis=1)
    gathered = lax.all_gather(packed, ("seq", "head"), axis=1, tiled=False)
    gathered = gathered.reshape(batch, n_seq, n_head, 2 * slab_sites + 8, width)
    donor_total = jnp.zeros((batch, n_seq, slab_sites, width), jnp.float32)
    acceptor_total = jnp.zeros((batch, n_seq, slab_sites, width), jnp.float32)
    for h in range(n_head):
        donor_total = donor_total + gathered[:, :, h, :slab_sites].astype(jnp.float32)
        acceptor_total = acceptor_total + gathered[:, :, h, slab_sites : 2 * slab_sites].astype(
            jnp.float32
        )
    donor_feat_all = donor_total.astype(jnp.bfloat16).reshape(batch, sites, width)
    acceptor_feat_all = acceptor_total.astype(jnp.bfloat16).reshape(batch, sites, width)
    donor_ok_all = (gathered[:, :, 0, 2 * slab_sites, :slab_sites] > 0).reshape(batch, sites)
    acceptor_ok_all = (gathered[:, :, 0, 2 * slab_sites + 1, :slab_sites] > 0).reshape(batch, sites)
    site_slab = jnp.arange(sites, dtype=jnp.int32) // slab_sites
    big = jnp.int32(1 << 30)
    acceptor_tiled = jnp.tile(acceptor_pos, (1, n_seq))
    acceptor_eff = jnp.where(
        site_slab[None, :] == slab,
        acceptor_tiled,
        jnp.where((site_slab[None, :] > slab) & acceptor_ok_all, (slab + 1) * slab_rows, -1),
    )
    donor_tiled = jnp.tile(donor_pos, (1, n_seq))
    donor_eff = jnp.where(
        site_slab[None, :] == slab,
        donor_tiled,
        jnp.where(
            site_slab[None, :] > slab, big, jnp.where(donor_ok_all, slab * slab_rows - 1, -1)
        ),
    )
    donor_feat = lax.dynamic_slice_in_dim(donor_feat_all, slab * slab_sites, slab_sites, 1)
    acceptor_feat = lax.dynamic_slice_in_dim(acceptor_feat_all, slab * slab_sites, slab_sites, 1)
    scores_row = (
        jnp.einsum(
            "bip,bjp->bij", donor_feat, acceptor_feat_all, preferred_element_type=jnp.float32
        )
        * scale
    )
    allowed_row = (donor_pos[:, :, None] >= 0) & (acceptor_eff[:, None, :] > donor_pos[:, :, None])
    slope_row = pair_slope(scores_row, target, allowed_row)
    donor_grad = (
        jnp.einsum("bij,bjp->bip", slope_row, acceptor_feat_all, preferred_element_type=jnp.float32)
        * scale
    ).astype(jnp.bfloat16)
    target_col = lax.dynamic_slice_in_dim(target_all, slab * slab_sites, slab_sites, 2)
    scores_col = (
        jnp.einsum(
            "bip,bjp->bij", donor_feat_all, acceptor_feat, preferred_element_type=jnp.float32
        )
        * scale
    )
    allowed_col = (donor_eff[:, :, None] >= 0) & (acceptor_pos[:, None, :] > donor_eff[:, :, None])
    slope_col = pair_slope(scores_col, target_col, allowed_col)
    acceptor_grad = (
        jnp.einsum("bij,bip->bjp", slope_col, donor_feat_all, preferred_element_type=jnp.float32)
        * scale
    ).astype(jnp.bfloat16)
    donor_site = jnp.einsum("bnp,cp->bnc", donor_grad, donor_w, preferred_element_type=jnp.float32)
    acceptor_site = jnp.einsum(
        "bnp,cp->bnc", acceptor_grad, acceptor_w, preferred_element_type=jnp.float32
    )
    row_grad = place_rows(donor_match, donor_site) + place_rows(acceptor_match, acceptor_site)
    local_dw = jnp.einsum("bnc,bnp->cp", donor_rows, donor_grad, preferred_element_type=jnp.float32)
    local_aw = jnp.einsum(
        "bnc,bnp->cp", acceptor_rows, acceptor_grad, preferred_element_type=jnp.float32
    )
    summed = lax.psum(jnp.stack([local_dw, local_aw]).astype(jnp.bfloat16), ("dp", "seq"))
    part = width // n_seq
    mine = lax.dynamic_slice_in_dim(summed, slab * part, part, 2).astype(jnp.float32)
    return (row_grad.astype(jnp.bfloat16), mine[0], mine[1])


def solution(mesh):
    in_specs = (
        P("dp", "seq", "head"),
        P("dp", "seq"),
        P("dp", "seq"),
        P("dp", "seq", None),
        P("head", None),
        P("head", None),
    )
    out_specs = (P("dp", "seq", "head"), P("head", "seq"), P("head", "seq"))
    return jax.shard_map(shards, mesh=mesh, in_specs=in_specs, out_specs=out_specs, check_vma=False)
```

profile of v0, /device:TPU:0, one launch (start us, length us, event | category | flops | bytes accessed | tf_op | source)
XLA Modules:
  0.0 129.9 jit_solution(11049242850485408550)
XLA Ops:
  7.2 0.0 copy-start
  7.2 0.0 copy-start.5
  7.2 0.0 copy-start.3
  7.2 0.0 all-gather.3.cloned.1.call-start
  7.3 0.7 compare_bitcast_fusion
  8.0 0.7 subtract_bitcast_fusion
  8.7 0.0 copy-done
  8.7 0.3 convolution_convert_fusion.3
  8.9 0.3 convolution_convert_fusion.5
  9.2 1.2 fusion.8
  10.4 0.0 copy-start.4
  10.4 1.2 fusion.7
  11.6 0.2 scatter.14
  11.8 0.7 pad_maximum_fusion.1
  12.5 0.0 all-gather.3.cloned.1.call-update
  12.5 0.0 all-reduce.3.cloned.1.call-start
  12.5 0.0 copy-done.3
  12.6 5.9 %all_gather.11 = bf16[1,256,256]{2,1,0:T(8,128)(2,1)S(1)} all-gather(bf16[1,128,256]{2,1,0:T(8,128)(2,1)S(1)} %copy-done.3), channel_id=1, replica_groups=mesh['dp'=4,'seq'=2,'head'=4] {'seq'}, dimensions={1}, use_global_device_ids=true | all-gather | bytes 196608 | tf_op jit(solution)/shard_map/all_gather | solution.py:36
  18.4 0.0 copy-done.5
  18.4 41.4 %all-gather.3.cloned.1.call-done = bf16[8,264,384]{2,1,0:T(8,128)(2,1)} async-done(((bf16[1,264,384]{2,1,0:T(8,128)(2,1)}), bf16[8,264,384]{2,1,0:T(8,128)(2,1)}) %all-gather.3.cloned.1.call-update) | async-done | bytes 1622032 | tf_op jit(solution)/shard_map/all_gather | solution.py:56
  59.8 0.0 copy-start.1
  59.8 1.7 %add_convert_fusion.1 = (bf16[1,2,1,128,384]{4,3,2,1,0:T(8,128)(2,1)S(1)}, bf16[1,2,1,128,384]{4,3,2,1,0:T(8,128)(2,1)S(1)}) fusion(bf16[1,2,4,264,384]{4,3,2,1,0:T(8,128)(2,1)} %bitcast.139), kind=kLoop, calls=%fused_computation.28 | loop fusion | flops 1572864 | bytes 1966080 | tf_op jit(solution)/shard_map/convert.9
  61.5 0.8 fusion.91
  62.3 0.0 copy-done.4
  62.3 0.6 fusion.6
  62.8 0.0 copy-done.1
  62.8 0.0 copy-start.2
  62.9 0.2 fusion.93
  63.1 0.3 fusion.4
  63.4 0.5 fusion.5
  63.9 0.0 copy-done.2
  63.9 0.2 fusion.92
  64.2 0.3 fusion.3
  64.4 0.4 fusion.12
  64.8 0.4 convolution_add_fusion.1
  65.2 0.9 pad_maximum_fusion
  66.1 0.0 all-reduce.3.cloned.1.call-update
  66.1 0.4 fusion.11
  66.5 1.1 fusion.2
  67.6 52.4 %all-reduce.3.cloned.1.call-done = bf16[2,384,384]{2,1,0:T(8,128)(2,1)} async-done(((bf16[2,384,384]{2,1,0:T(8,128)(2,1)}), bf16[2,384,384]{2,1,0:T(8,128)(2,1)}) %all-reduce.3.cloned.1.call-update) | async-done | bytes 589840 | tf_op jit(solution)/shard_map/psum | solution.py:121
  120.0 1.2 dynamic-slice_convert_fusion
  121.3 0.1 slice_bitcast_fusion
  121.3 0.9 copy.17
  122.2 0.9 copy.18
  (4 shorter events, 0.0 us)
Async XLA Ops:
  7.2 1.5 %copy-start = (bf16[1,512,384]{2,1,0:T(8,128)(2,1)S(1)}, bf16[1,512,384]{2,1,0:T(8,128)(2,1)}, u32[]{:S(2)}) copy-start(bf16[1,512,384]{2,1,0:T(8,128)(2,1)} %param.10) | copy-start | bytes 1179652
  7.2 11.2 %copy-start.5 = (s32[1,128]{1,0:T(1,128)S(1)}, s32[1,128]{1,0:T(1,128)}, u32[]{:S(2)}) copy-start(s32[1,128]{1,0:T(1,128)} %param.11) | copy-start | bytes 1540
  7.2 5.4 %copy-start.3 = (bf16[1,128,256]{2,1,0:T(8,128)(2,1)S(1)}, bf16[1,128,256]{2,1,0:T(8,128)(2,1)}, u32[]{:S(2)}) copy-start(bf16[1,128,256]{2,1,0:T(8,128)(2,1)} %param.13) | copy-start | bytes 196612
  7.2 52.6 %all-gather.3.cloned.1.call-start = ((), (), s32[]{:S(2)}) async-start(), calls=%async_computation.1 | async-start | bytes 1824768 | tf_op jit(solution)/shard_map/all_gather | solution.py:56
  10.4 51.9 %copy-start.4 = (s32[1,128]{1,0:T(1,128)S(1)}, s32[1,128]{1,0:T(1,128)}, u32[]{:S(2)}) copy-start(s32[1,128]{1,0:T(1,128)} %param.12) | copy-start | bytes 1540
  12.5 107.5 %all-reduce.3.cloned.1.call-start = ((), (), s32[]{:S(2)}) async-start(), calls=%async_computation | async-start | bytes 1179648 | tf_op jit(solution)/shard_map/psum | solution.py:121
  59.8 3.0 %copy-start.1 = (bf16[384,384]{1,0:T(8,128)(2,1)S(1)}, bf16[384,384]{1,0:T(8,128)(2,1)}, u32[]{:S(2)}) copy-start(bf16[384,384]{1,0:T(8,128)(2,1)} %param.15) | copy-start | bytes 884740
  62.8 1.1 copy-start.2
Sparse Core Ops, SparseCore 0:
  12.6 47.1 all-gather.2
  66.2 53.7 all-reduce.2
where the time goes:
time: 130 us
  waiting for transfers between devices  93.8 us (72%)
  between operations  14.2 us (11%)
  matrix products  7.21 us (6%)
  other arithmetic  5.94 us (5%)
  blocking collectives  5.86 us (5%)
  local copies, waits for them, and re-layouts  2.75 us (2%)
    psum x1, waiting for transfers between devices, shards(): lax.psum(jnp.stack([local_dw, local_aw]).astype(jnp.bfloat16), ('dp', 'se...  52.4 us
    all_gather x1, waiting for transfers between devices, shards(): gathered = lax.all_gather(packed, ('seq', 'head'), axis=1, tiled=False)  41.4 us
    all_gather x1, blocking collectives, shards(): target_all = lax.all_gather(target, 'seq', axis=1, tiled=True)  5.86 us
  transfers between devices with their start and end apart: 2, of which 2 were waited for; matrix products, arithmetic and copies ran while one was open for 1% of the time, Pallas kernels for 0%

commit v1 on v0

--- a/solution.py
+++ b/solution.py
@@ -118,7 +118,9 @@
     local_aw = jnp.einsum(
         "bnc,bnp->cp", acceptor_rows, acceptor_grad, preferred_element_type=jnp.float32
     )
-    summed = lax.psum(jnp.stack([local_dw, local_aw]).astype(jnp.bfloat16), ("dp", "seq"))
+    summed = jnp.sum(
+        lax.all_gather(jnp.stack([local_dw, local_aw]).astype(jnp.bfloat16), ("dp", "seq")), axis=0
+    )
     part = width // n_seq
     mine = lax.dynamic_slice_in_dim(summed, slab * part, part, 2).astype(jnp.float32)
     return (row_grad.astype(jnp.bfloat16), mine[0], mine[1])

time: 130 us -> 115 us (0.88)
  waiting for transfers between devices: 93.8 us -> 76.5 us
  other arithmetic: 5.94 us -> 8.05 us
    psum x1 -> x0, waiting for transfers between devices: 52.4 us -> none  [shards(): lax.psum(jnp.stack([local_dw, local_aw]).astype(jnp.bfloat16), ('dp', 'se...]
    all_gather x0 -> x1, waiting for transfers between devices: none -> 35.1 us  [shards(): lax.all_gather(jnp.stack([local_dw, local_aw]).astype(jnp.bfloat16), ('dp...]
    reduce_sum x0 -> x1, other arithmetic: none -> 3.18 us  [shards(): jnp.sum(lax.all_gather(jnp.stack([local_dw, local_aw]).astype(jnp.bfloat1...]
  transfers between devices with their start and end apart: 2 -> 2, of which waited for: 2 -> 2; matrix products, arithmetic and copies ran while one was open for 1% -> 2% of each run, Pallas kernels for 0% -> 0%
where the time goes in v1:
time: 115 us
  waiting for transfers between devices  76.5 us (67%)
  between operations  14.3 us (12%)
  other arithmetic  8.05 us (7%)
  matrix products  7.21 us (6%)
  blocking collectives  5.86 us (5%)
  local copies, waits for them, and re-layouts  2.75 us (2%)
    all_gather x1, waiting for transfers between devices, shards(): gathered = lax.all_gather(packed, ('seq', 'head'), axis=1, tiled=False)  41.4 us
    all_gather x1, waiting for transfers between devices, shards(): lax.all_gather(jnp.stack([local_dw, local_aw]).astype(jnp.bfloat16), ('dp...  35.1 us
    all_gather x1, blocking collectives, shards(): target_all = lax.all_gather(target, 'seq', axis=1, tiled=True)  5.86 us
    reduce_sum x1, other arithmetic, shards(): jnp.sum(lax.all_gather(jnp.stack([local_dw, local_aw]).astype(jnp.bfloat1...  3.18 us
    another operation x2, other arithmetic  2.39 us
  transfers between devices with their start and end apart: 2, of which 2 were waited for; matrix products, arithmetic and copies ran while one was open for 2% of the time, Pallas kernels for 0%

profile of v1, /device:TPU:0, one launch (start us, length us, event | category | flops | bytes accessed | tf_op | source)
XLA Modules:
  0.0 114.7 jit_solution(15813703713643450030)
XLA Ops:
  7.2 0.0 copy-start
  7.2 0.0 copy-start.5
  7.2 0.0 copy-start.3
  7.2 0.0 all-gather.6.cloned.1.call-start
  7.3 0.7 compare_bitcast_fusion
  8.0 0.7 subtract_bitcast_fusion
  8.7 0.0 copy-done
  8.7 0.3 convolution_convert_fusion.5
  8.9 0.3 convolution_convert_fusion.3
  9.2 1.2 %fusion.7 = bf16[1,128,384]{2,1,0:T(8,128)(2,1)S(1)} fusion(bf16[128,384]{1,0:T(8,128)(2,1)S(1)} %convolution_convert_fusion.5, bf16[384,384]{1,0:T(8,128)(2,1)} %param.14), kind=kOutput, calls=%fused_computation.19 | convolution fusion | flops 37797888 | bytes 491520 | tf_op jit(solution)/shard_map/bnc,cp->bnp/dot_general | solution.py:45
  10.4 0.0 copy-start.4
  10.4 1.2 %fusion.8 = bf16[1,128,384]{2,1,0:T(8,128)(2,1)S(1)} fusion(bf16[128,384]{1,0:T(8,128)(2,1)S(1)} %convolution_convert_fusion.3, bf16[384,384]{1,0:T(8,128)(2,1)} %param.15), kind=kOutput, calls=%fused_computation.20 | convolution fusion | flops 37797888 | bytes 491520 | tf_op jit(solution)/shard_map/bnc,cp->bnp/dot_general | solution.py:48
  11.6 0.2 scatter.14
  11.8 0.7 pad_maximum_fusion.1
  12.5 0.0 all-gather.6.cloned.1.call-update
  12.5 0.0 all-gather.4.cloned.1.call-start
  12.5 0.0 copy-done.3
  12.6 5.9 %all_gather.15 = bf16[1,256,256]{2,1,0:T(8,128)(2,1)S(1)} all-gather(bf16[1,128,256]{2,1,0:T(8,128)(2,1)S(1)} %copy-done.3), channel_id=1, replica_groups=mesh['dp'=4,'seq'=2,'head'=4] {'seq'}, dimensions={1}, use_global_device_ids=true | all-gather | bytes 196608 | tf_op jit(solution)/shard_map/all_gather | solution.py:36
  18.4 0.0 copy-done.5
  18.4 41.4 %all-gather.6.cloned.1.call-done = bf16[8,264,384]{2,1,0:T(8,128)(2,1)} async-done(((bf16[1,264,384]{2,1,0:T(8,128)(2,1)}), bf16[8,264,384]{2,1,0:T(8,128)(2,1)}) %all-gather.6.cloned.1.call-update) | async-done | bytes 1622032 | tf_op jit(solution)/shard_map/all_gather | solution.py:56
  59.8 0.8 fusion.91
  60.6 1.7 %add_convert_fusion.1 = (bf16[1,2,1,128,384]{4,3,2,1,0:T(8,128)(2,1)S(1)}, bf16[1,2,1,128,384]{4,3,2,1,0:T(8,128)(2,1)S(1)}) fusion(bf16[1,2,4,264,384]{4,3,2,1,0:T(8,128)(2,1)} %bitcast.140), kind=kLoop, calls=%fused_computation.28 | loop fusion | flops 1572864 | bytes 1966080 | tf_op jit(solution)/shard_map/convert.10
  62.2 0.0 copy-done.4
  62.3 0.6 fusion.6
  62.8 0.3 fusion.4
  63.1 0.5 fusion.5
  63.6 0.0 copy-start.1
  63.6 0.0 copy-start.2
  63.7 0.3 fusion.3
  63.9 0.9 pad_maximum_fusion
  64.8 0.0 all-gather.4.cloned.1.call-update
  64.8 0.0 copy-done.1
  64.8 0.2 fusion.93
  65.1 0.0 copy-done.2
  65.1 0.2 fusion.92
  65.3 0.4 fusion.11
  65.7 0.4 fusion.12
  66.1 0.4 convolution_add_fusion.1
  66.5 1.1 fusion.2
  67.6 35.1 %all-gather.4.cloned.1.call-done = bf16[8,2,384,384]{3,2,1,0:T(8,128)(2,1)} async-done(((bf16[1,2,384,384]{3,2,1,0:T(8,128)(2,1)}), bf16[8,2,384,384]{3,2,1,0:T(8,128)(2,1)}) %all-gather.4.cloned.1.call-update) | async-done | bytes 4718608 | tf_op jit(solution)/shard_map/all_gather | solution.py:122
  102.7 3.2 %reduce_sum.12 = bf16[2,384,384]{2,1,0:T(8,128)(2,1)S(1)} reduce(bf16[8,2,384,384]{3,2,1,0:T(8,128)(2,1)} %all-gather.4.cloned.1.call-done, bf16[]{:T(256)} %constant.115.clone.1), dimensions={0}, to_apply=%region_0.0 | reduce | flops 2064384 | bytes 5308418 | tf_op jit(solution)/shard_map/reduce_sum | solution.py:121
  105.9 0.2 dynamic-slice_convert_fusion
  106.1 0.1 slice_bitcast_fusion
  106.2 0.9 copy.13
  107.0 0.9 copy.14
  (4 shorter events, 0.0 us)
Async XLA Ops:
  7.2 1.5 %copy-start = (bf16[1,512,384]{2,1,0:T(8,128)(2,1)S(1)}, bf16[1,512,384]{2,1,0:T(8,128)(2,1)}, u32[]{:S(2)}) copy-start(bf16[1,512,384]{2,1,0:T(8,128)(2,1)} %param.10) | copy-start | bytes 1179652
  7.2 11.2 %copy-start.5 = (s32[1,128]{1,0:T(1,128)S(1)}, s32[1,128]{1,0:T(1,128)}, u32[]{:S(2)}) copy-start(s32[1,128]{1,0:T(1,128)} %param.11) | copy-start | bytes 1540
  7.2 5.4 %copy-start.3 = (bf16[1,128,256]{2,1,0:T(8,128)(2,1)S(1)}, bf16[1,128,256]{2,1,0:T(8,128)(2,1)}, u32[]{:S(2)}) copy-start(bf16[1,128,256]{2,1,0:T(8,128)(2,1)} %param.13) | copy-start | bytes 196612
  7.2 52.6 %all-gather.6.cloned.1.call-start = ((), (), s32[]{:S(2)}) async-start(), calls=%async_computation.1 | async-start | bytes 1824768 | tf_op jit(solution)/shard_map/all_gather | solution.py:56
  10.4 51.9 %copy-start.4 = (s32[1,128]{1,0:T(1,128)S(1)}, s32[1,128]{1,0:T(1,128)}, u32[]{:S(2)}) copy-start(s32[1,128]{1,0:T(1,128)} %param.12) | copy-start | bytes 1540
  12.5 90.2 %all-gather.4.cloned.1.call-start = ((), (), s32[]{:S(2)}) async-start(), calls=%async_computation | async-start | bytes 5308416 | tf_op jit(solution)/shard_map/all_gather | solution.py:122
  63.6 1.2 %copy-start.1 = (bf16[384,384]{1,0:T(8,128)(2,1)S(1)}, bf16[384,384]{1,0:T(8,128)(2,1)}, u32[]{:S(2)}) copy-start(bf16[384,384]{1,0:T(8,128)(2,1)} %param.15) | copy-start | bytes 884740
  63.6 1.4 %copy-start.2 = (bf16[384,384]{1,0:T(8,128)(2,1)S(1)}, bf16[384,384]{1,0:T(8,128)(2,1)}, u32[]{:S(2)}) copy-start(bf16[384,384]{1,0:T(8,128)(2,1)} %param.14) | copy-start | bytes 884740
Sparse Core Ops, SparseCore 0:
  12.6 47.1 all-gather.5
  65.0 37.7 all-gather.3

commit v2 on v0

--- a/solution.py
+++ b/solution.py
@@ -118,7 +118,7 @@
     local_aw = jnp.einsum(
         "bnc,bnp->cp", acceptor_rows, acceptor_grad, preferred_element_type=jnp.float32
     )
-    summed = lax.psum(jnp.stack([local_dw, local_aw]).astype(jnp.bfloat16), ("dp", "seq"))
+    summed = lax.psum(lax.psum(jnp.stack([local_dw, local_aw]).astype(jnp.bfloat16), "seq"), "dp")
     part = width // n_seq
     mine = lax.dynamic_slice_in_dim(summed, slab * part, part, 2).astype(jnp.float32)
     return (row_grad.astype(jnp.bfloat16), mine[0], mine[1])

time: 130 us -> 140 us (1.077)
  waiting for transfers between devices: 93.8 us -> 104 us
    psum x1 -> x2, waiting for transfers between devices: 52.4 us -> 62.3 us  [the longest x1 34.4 us: shards(): lax.psum(lax.psum(jnp.stack([local_dw, local_aw]).astype(jnp.bfloat16), '...]
  transfers between devices with their start and end apart: 2 -> 3, of which waited for: 2 -> 3; matrix products, arithmetic and copies ran while one was open for 1% -> 2% of each run, Pallas kernels for 0% -> 0%
where the time goes in v2:
time: 140 us
  waiting for transfers between devices  104 us (74%)
  between operations  13.9 us (10%)
  matrix products  7.22 us (5%)
  other arithmetic  5.94 us (4%)
  blocking collectives  5.86 us (4%)
  local copies, waits for them, and re-layouts  2.75 us (2%)
    all_gather x1, waiting for transfers between devices, shards(): gathered = lax.all_gather(packed, ('seq', 'head'), axis=1, tiled=False)  41.4 us
    psum x1, waiting for transfers between devices, shards(): lax.psum(lax.psum(jnp.stack([local_dw, local_aw]).astype(jnp.bfloat16), '...  34.4 us
    psum x1, waiting for transfers between devices, shards(): lax.psum(jnp.stack([local_dw, local_aw]).astype(jnp.bfloat16), 'seq')  27.9 us
    all_gather x1, blocking collectives, shards(): target_all = lax.all_gather(target, 'seq', axis=1, tiled=True)  5.86 us
  transfers between devices with their start and end apart: 3, of which 3 were waited for; matrix products, arithmetic and copies ran while one was open for 2% of the time, Pallas kernels for 0%

profile of v2, /device:TPU:0, one launch (start us, length us, event | category | flops | bytes accessed | tf_op | source)
XLA Modules:
  0.0 139.6 jit_solution(9079687397158841948)
XLA Ops:
  7.2 0.0 copy-start
  7.2 0.0 copy-start.5
  7.2 0.0 copy-start.3
  7.2 0.0 all-gather.3.cloned.1.call-start
  7.3 0.7 compare_bitcast_fusion
  8.0 0.7 subtract_bitcast_fusion
  8.7 0.0 copy-done
  8.7 0.3 convolution_convert_fusion.3
  8.9 0.3 convolution_convert_fusion.5
  9.2 1.2 fusion.8
  10.4 0.0 copy-start.4
  10.4 1.2 fusion.7
  11.6 0.2 scatter.14
  11.8 0.7 pad_maximum_fusion.1
  12.5 0.0 all-gather.3.cloned.1.call-update
  12.5 0.0 all-reduce.4.cloned.1.call-start
  12.5 0.0 copy-done.3
  12.6 5.9 %all_gather.11 = bf16[1,256,256]{2,1,0:T(8,128)(2,1)S(1)} all-gather(bf16[1,128,256]{2,1,0:T(8,128)(2,1)S(1)} %copy-done.3), channel_id=1, replica_groups=mesh['dp'=4,'seq'=2,'head'=4] {'seq'}, dimensions={1}, use_global_device_ids=true | all-gather | bytes 196608 | tf_op jit(solution)/shard_map/all_gather | solution.py:36
  18.4 0.0 copy-done.5
  18.4 41.4 %all-gather.3.cloned.1.call-done = bf16[8,264,384]{2,1,0:T(8,128)(2,1)} async-done(((bf16[1,264,384]{2,1,0:T(8,128)(2,1)}), bf16[8,264,384]{2,1,0:T(8,128)(2,1)}) %all-gather.3.cloned.1.call-update) | async-done | bytes 1622032 | tf_op jit(solution)/shard_map/all_gather | solution.py:56
  59.8 0.0 copy-start.1
  59.8 1.7 %add_convert_fusion.1 = (bf16[1,2,1,128,384]{4,3,2,1,0:T(8,128)(2,1)S(1)}, bf16[1,2,1,128,384]{4,3,2,1,0:T(8,128)(2,1)S(1)}) fusion(bf16[1,2,4,264,384]{4,3,2,1,0:T(8,128)(2,1)} %bitcast.139), kind=kLoop, calls=%fused_computation.28 | loop fusion | flops 1572864 | bytes 1966080 | tf_op jit(solution)/shard_map/convert.9
  61.5 0.8 fusion.91
  62.3 0.0 copy-done.4
  62.3 0.5 fusion.5
  62.8 0.0 copy-done.1
  62.8 0.2 fusion.92
  63.0 0.3 fusion.3
  63.3 0.5 fusion.6
  63.9 0.0 copy-start.2
  63.9 0.3 fusion.4
  64.2 0.9 pad_maximum_fusion
  65.1 0.0 all-reduce.4.cloned.1.call-update
  65.1 0.0 all-reduce.6.cloned.1.call-start
  65.1 0.0 copy-done.2
  65.1 0.2 fusion.93
  65.4 0.4 fusion.12
  65.8 0.4 convolution_add_fusion.1
  66.1 27.9 %all-reduce.4.cloned.1.call-done = bf16[2,384,384]{2,1,0:T(8,128)(2,1)} async-done(((bf16[2,384,384]{2,1,0:T(8,128)(2,1)}), bf16[2,384,384]{2,1,0:T(8,128)(2,1)}) %all-reduce.4.cloned.1.call-update) | async-done | bytes 589840 | tf_op jit(solution)/shard_map/psum | solution.py:121
  94.1 0.0 all-reduce.6.cloned.1.call-update
  94.1 0.4 fusion.11
  94.5 1.1 fusion.2
  95.6 34.4 %all-reduce.6.cloned.1.call-done = bf16[2,384,384]{2,1,0:T(8,128)(2,1)} async-done(((bf16[2,384,384]{2,1,0:T(8,128)(2,1)}), bf16[2,384,384]{2,1,0:T(8,128)(2,1)}) %all-reduce.6.cloned.1.call-update) | async-done | bytes 589840 | tf_op jit(solution)/shard_map/psum | solution.py:121
  130.0 1.2 dynamic-slice_convert_fusion
  131.3 0.1 slice_bitcast_fusion
  131.3 0.9 copy.17
  132.2 0.9 copy.18
  (4 shorter events, 0.0 us)
Async XLA Ops:
  7.2 1.5 %copy-start = (bf16[1,512,384]{2,1,0:T(8,128)(2,1)S(1)}, bf16[1,512,384]{2,1,0:T(8,128)(2,1)}, u32[]{:S(2)}) copy-start(bf16[1,512,384]{2,1,0:T(8,128)(2,1)} %param.10) | copy-start | bytes 1179652
  7.2 11.2 %copy-start.5 = (s32[1,128]{1,0:T(1,128)S(1)}, s32[1,128]{1,0:T(1,128)}, u32[]{:S(2)}) copy-start(s32[1,128]{1,0:T(1,128)} %param.11) | copy-start | bytes 1540
  7.2 5.4 %copy-start.3 = (bf16[1,128,256]{2,1,0:T(8,128)(2,1)S(1)}, bf16[1,128,256]{2,1,0:T(8,128)(2,1)}, u32[]{:S(2)}) copy-start(bf16[1,128,256]{2,1,0:T(8,128)(2,1)} %param.13) | copy-start | bytes 196612
  7.2 52.6 %all-gather.3.cloned.1.call-start = ((), (), s32[]{:S(2)}) async-start(), calls=%async_computation.2 | async-start | bytes 1824768 | tf_op jit(solution)/shard_map/all_gather | solution.py:56
  10.4 51.9 %copy-start.4 = (s32[1,128]{1,0:T(1,128)S(1)}, s32[1,128]{1,0:T(1,128)}, u32[]{:S(2)}) copy-start(s32[1,128]{1,0:T(1,128)} %param.12) | copy-start | bytes 1540
  12.5 81.6 %all-reduce.4.cloned.1.call-start = ((), (), s32[]{:S(2)}) async-start(), calls=%async_computation | async-start | bytes 1179648 | tf_op jit(solution)/shard_map/psum | solution.py:121
  59.8 3.0 %copy-start.1 = (bf16[384,384]{1,0:T(8,128)(2,1)S(1)}, bf16[384,384]{1,0:T(8,128)(2,1)}, u32[]{:S(2)}) copy-start(bf16[384,384]{1,0:T(8,128)(2,1)} %param.14) | copy-start | bytes 884740
  63.9 1.2 copy-start.2
  65.1 65.0 %all-reduce.6.cloned.1.call-start = ((), (), s32[]{:S(2)}) async-start(), calls=%async_computation.1 | async-start | bytes 1179648 | tf_op jit(solution)/shard_map/psum | solution.py:121
Sparse Core Ops, SparseCore 0:
  12.6 47.1 all-gather.2
  65.2 28.8 all-reduce.3
  96.5 33.4 all-reduce.5
